TPU v7x, 256 devices: a whole 4x4x8 slice. The times are simulated.
256 devices in a mesh: row: 8 (over z), col: 32 (over y, x, core).
Axes of the slice: x: 4, y: 4, z: 8, core: 2. Of those that a mesh axis runs over, the one named last changes fastest.
Arguments:
- embeds: bfloat16 [24576, 768], P('col'), may hold values from -6 to 6
- labels: bfloat16 [24576, 1000], P('col'), may hold values from -6 to 6
- sharpness: float32 [24576], P('col'), may hold values from 0.5 to 100
- pattern: int32 [192, 16], P('col'), may hold values from 0 to 191, as said below
- mask_pos: int32 [24576, 50], P('col'), may hold values from 0 to 2047, as said below
Outputs:
- propagated: bfloat16 [24576, 1000], P('col', 'row')
Inputs may be any that keep to these rules, and one draw needn't show every extreme that they name: `pattern`: split the row blocks into runs of 6 and the slots into runs of 2; within one run of row blocks and one run of slots, ids that lie in the same run of 6 block ids are equal. `mask_pos`: the 50 positions of a row are distinct; position k * 128 + m names row m of the row block's k-th candidate block.
All inputs are finite; a program needn't handle non-finite values.
Results may differ from a plain program's by a relative error of at most 0.012.
Values may be sent and summed in bfloat16 or wider, within the bound.
No kernel may reach another device: no remote copies, remote signals or barrier semaphores. Data moves between devices by JAX's collectives and lax.ppermute only.
A program may use at most 128 MiB of HBM per device.

v0:
```python
import math
import jax
import jax.numpy as jnp
from jax import lax
from jax.sharding import PartitionSpec as P

BLOCK = 128
SLOTS = 16
mixing = 0.75
lowest_logit = -1e30
COL = ("chip", "core")


def gather_columns(x):
    rows_here, width = x.shape
    same_core = lax.all_gather(x, "chip", tiled=True).reshape(-1, BLOCK, width)
    other_core = lax.ppermute(same_core, "core", [(0, 1), (1, 0)])
    return (same_core, other_core)


def body(embeds, labels, sharpness, pattern, mask_pos):
    rows_here, width = embeds.shape
    classes = labels.shape[1]
    n_col = lax.axis_size(COL)
    n_row = lax.axis_size("row")
    row_pos = lax.axis_index("row")
    blocks_here = rows_here // BLOCK
    slots_here = SLOTS // n_row
    span = slots_here * BLOCK
    per_device = classes // n_row
    owners = pattern // blocks_here
    local_ids = pattern % blocks_here
    my_owners = lax.dynamic_slice_in_dim(owners, row_pos * slots_here, slots_here, 1)
    my_ids = lax.dynamic_slice_in_dim(local_ids, row_pos * slots_here, slots_here, 1)
    peers = jnp.arange(n_col, dtype=jnp.int32)
    wanted = jnp.max(jnp.where(my_owners[..., None] == peers, my_ids[..., None], 0), axis=(0, 1))
    requested = lax.all_to_all(wanted, COL, split_axis=0, concat_axis=0, tiled=True)
    embedding_tiles = embeds.reshape(blocks_here, BLOCK, width)
    send_emb = embedding_tiles[requested]
    my_labels = lax.dynamic_slice_in_dim(labels, row_pos * per_device, per_device, 1)
    lanes = -(-per_device // 128) * 128
    my_labels = jnp.pad(my_labels, ((0, 0), (0, lanes - per_device)))
    all_labels = gather_columns(my_labels)
    shifted = mask_pos - row_pos * span
    shifted = jnp.where((shifted >= 0) & (shifted < span), shifted, span)
    positions = jnp.arange(span, dtype=jnp.int32)
    in_mask = jnp.any(shifted[:, :, None] == positions[None, None, :], axis=1)
    in_mask = in_mask.reshape(blocks_here, BLOCK, span)
    fetched_emb = lax.all_to_all(send_emb, COL, split_axis=0, concat_axis=0, tiled=True)
    candidate_ids = fetched_emb[my_owners].reshape(blocks_here, span, width)
    scores = jnp.einsum(
        "evg,erg->evr", embedding_tiles, candidate_ids, preferred_element_type=jnp.float32
    ) / math.sqrt(width)
    logits = scores * sharpness.reshape(blocks_here, BLOCK, 1)
    local_max = jnp.max(jnp.where(in_mask, logits, lowest_logit), axis=2)
    local_sum = jnp.sum(jnp.where(in_mask, jnp.exp(logits - local_max[..., None]), 0.0), axis=2)
    local_weights = jnp.where(in_mask, jnp.exp(logits - local_max[..., None]), 0.0).astype(
        jnp.bfloat16
    )
    stats = lax.all_gather(jnp.stack([local_max, local_sum]), "row")
    all_weights = lax.all_gather(local_weights, "row")
    top = jnp.max(stats[:, 0], axis=0)
    totals = jnp.sum(stats[:, 1] * jnp.exp(stats[:, 0] - top), axis=0)
    factors = jnp.exp(stats[:, 0] - top) / totals
    shard_of = pattern // blocks_here
    on_this_core = (shard_of % 2 == lax.axis_index("core"))[..., None, None]
    pair_ids = shard_of // 2 * blocks_here + pattern % blocks_here

    def propagate_using(gathered, seed, whole=False):
        if whole:
            candidates = gathered[pattern]
        else:
            same_core, other_core = gathered
            candidates = jnp.where(on_this_core, same_core[pair_ids], other_core[pair_ids])
        candidates = candidates.reshape(blocks_here, n_row, span, lanes)
        pieces = jnp.einsum(
            "gtmk,tgkc->gtmc", all_weights, candidates, preferred_element_type=jnp.float32
        )
        pieces = (pieces * factors[..., None]).astype(jnp.bfloat16)
        summed = jnp.sum(pieces.astype(jnp.float32), axis=0).reshape(rows_here, lanes)
        return (mixing * summed + (1.0 - mixing) * seed.astype(jnp.float32)).astype(jnp.bfloat16)

    spread = propagate_using(all_labels, my_labels)
    whole_spread = lax.all_gather(spread, COL, tiled=True).reshape(-1, BLOCK, lanes)
    return propagate_using(whole_spread, my_labels, whole=True)[:, :per_device]


def solution(mesh):
    devices = mesh.devices
    fine = jax.sharding.Mesh(
        devices.reshape(devices.shape[0], devices.shape[1] // 2, 2), ("row", "chip", "core")
    )
    placed = (P(COL, None), P(COL, None), P(COL), P(COL, None), P(COL, None))
    return jax.shard_map(body, mesh=fine, in_specs=placed, out_specs=P(COL, "row"), check_vma=False)
```

profile of v0, /device:TPU:1, one launch (start us, length us, event | category | flops | bytes accessed | tf_op | source)
XLA Modules:
  0.0 252.2 jit_solution(4640348290725915735)
XLA Ops:
  6.5 0.0 copy-start
  6.5 0.8 fusion.23
  7.4 0.7 compare_select_fusion.1
  8.1 0.1 compare_select_fusion.3
  8.1 0.1 fusion.22
  8.2 0.1 copy.42
  8.3 15.3 %all_to_all.17 = s32[32,1,1]{2,1,0:T(1,128)S(1)} all-to-all(s32[32,1,1]{2,1,0:T(1,128)S(1)} %copy.42), channel_id=1, replica_groups=mesh['row'=8,'chip'=16,'core'=2] {'chip','core'}, dimensions={0} | all-to-all | bytes 256 | tf_op jit(solution)/shard_map/all_to_all | solution.py:37
  23.7 0.7 reduce.1
  24.4 4.9 %gather_fusion = bf16[32,128,768]{2,1,0:T(8,128)(2,1)} fusion(bf16[6,128,768]{2,1,0:T(8,128)(2,1)} %bitcast.49, s32[1024]{0:T(1024)S(1)} %pad_clamp_fusion.3), kind=kCustom, calls=%fused_computation | custom fusion | bytes 12583040 | tf_op jit(solution)/shard_map/gather | solution.py:39
  29.2 5.3 %all-to-all-start.1 = ((bf16[32,128,768]{2,1,0:T(8,128)(2,1)}), bf16[32,128,768]{2,1,0:T(8,128)(2,1)}, u32[]{:S(2)}, u32[]{:S(2)}) async-start(bf16[32,128,768]{2,1,0:T(8,128)(2,1)} %gather_fusion), calls=%async_computation.1 | async-start | bytes 12582912 | tf_op jit(solution)/shard_map/all_to_all | solution.py:49
  34.5 0.0 all-gather.6.cloned.1.call-start
  34.6 0.0 copy-done
  34.6 0.1 constant_dynamic-slice_fusion
  34.6 0.2 copy.51
  34.8 0.0 copy-start.1
  34.8 0.7 pad.4
  35.5 0.0 all-gather.6.cloned.1.call-update
  35.6 0.0 all-gather.10.cloned.1.call-start
  35.6 0.0 copy-done.2
  35.7 7.2 %fusion = pred[768,256]{1,0:T(8,128)(4,1)S(1)} fusion(s32[768,50]{0,1:T(8,128)S(1)} %and_select_fusion), kind=kLoop, calls=%fused_computation.6 | loop fusion | flops 19464192 | bytes 350208 | tf_op jit(solution)/shard_map/reduce_or | solution.py:47
  42.9 0.3 copy.44
  43.2 0.1 reshape.92
  43.3 0.0 copy-done.3
  43.3 68.2 %all-to-all-done.1 = bf16[32,128,768]{2,1,0:T(8,128)(2,1)} async-done(((bf16[32,128,768]{2,1,0:T(8,128)(2,1)}), bf16[32,128,768]{2,1,0:T(8,128)(2,1)}, u32[]{:S(2)}, u32[]{:S(2)}) %all-to-all-start.1) | async-done | bytes 6291488 | tf_op jit(solution)/shard_map/all_to_all | solution.py:49
  111.5 5.2 %gather_fusion.1 = bf16[12,128,768]{2,1,0:T(8,128)(2,1)} fusion(bf16[32,128,768]{2,1,0:T(8,128)(2,1)} %all-to-all-done.1, s32[1024]{0:T(1024)S(1)} %pad_clamp_fusion.2), kind=kCustom, calls=%fused_computation.1 | custom fusion | bytes 4718640 | tf_op jit(solution)/shard_map/gather | solution.py:50
  116.8 0.0 copy-done.1
  116.8 2.5 select_reduce_fusion
  119.3 0.2 fusion.15
  119.5 1.0 copy.45
  120.4 0.0 all-gather.10.cloned.1.call-update
  120.5 0.0 all-gather.8.cloned.1.call-start
  120.5 8.6 %all-gather.6.cloned.1.call-done = bf16[12288,128]{1,0:T(8,128)(2,1)} async-done(((bf16[768,128]{1,0:T(8,128)(2,1)}), bf16[12288,128]{1,0:T(8,128)(2,1)}) %all-gather.6.cloned.1.call-update) | async-done | bytes 3145744 | tf_op jit(solution)/shard_map/all_gather | solution.py:16
  129.1 1.3 collective-permute-start
  130.4 0.1 reshape.100
  130.5 0.1 broadcast_in_dim.63
  130.6 4.6 %gather_fusion.2 = bf16[96,128,128]{2,1,0:T(8,128)(2,1)} fusion(bf16[96,128,128]{2,1,0:T(8,128)(2,1)} %bitcast.52, s32[1024]{0:T(1024)S(1)} %pad_clamp_fusion.1), kind=kCustom, calls=%fused_computation.2 | custom fusion | bytes 6291840 | tf_op jit(solution)/shard_map/gather | solution.py:74
  135.2 22.3 %all-gather.1 = f32[16,6,128]{2,1,0:T(8,128)S(1)} all-gather(f32[2,6,128]{2,1,0:T(8,128)S(1)} %pad_maximum_fusion), channel_id=3, replica_groups=mesh['row'=8,'chip'=16,'core'=2] {'row'}, dimensions={0}, use_global_device_ids=true | all-gather | bytes 55296 | tf_op jit(solution)/shard_map/all_gather | solution.py:60
  157.6 0.0 collective-permute-done
  157.6 4.7 %gather_fusion.3 = bf16[96,128,128]{2,1,0:T(8,128)(2,1)} fusion(bf16[96,128,128]{2,1,0:T(8,128)(2,1)} %collective-permute-done, s32[1024]{0:T(1024)S(1)} %pad_clamp_fusion.1), kind=kCustom, calls=%fused_computation.3 | custom fusion | bytes 6291840 | tf_op jit(solution)/shard_map/gather | solution.py:74
  162.3 13.1 %all-gather.10.cloned.1.call-done = bf16[48,128,256]{2,1,0:T(8,128)(2,1)} async-done(((bf16[6,128,256]{2,1,0:T(8,128)(2,1)}), bf16[48,128,256]{2,1,0:T(8,128)(2,1)}) %all-gather.10.cloned.1.call-update) | async-done | bytes 3145744 | tf_op jit(solution)/shard_map/all_gather | solution.py:61
  175.4 5.9 %convert_reduce_fusion.1 = f32[6,128,128]{2,1,0:T(8,128)S(1)} fusion(f32[8,6,128]{2,1,0:T(8,128)S(1)} %fusion.21, bf16[8,6,128,256]{3,2,1,0:T(8,128)(2,1)} %bitcast.66, bf16[6,8,256,128]{3,2,1,0:T(8,128)(2,1)} %bitcast.53, bf16[6,8,256,128]{3,2,1,0:T(8,128)(2,1)} %bitcast.54, pred[6,8,256]{2,1,0:T(8,128)(4,1)S(1)} %broadcast_in_dim.64), kind=kOutput, calls=%fused_computation.13 | convolution fusion | flops 407273472 | bytes 9867264 | tf_op jit(solution)/shard_map/gtmk,tgkc->gtmc/dot_general | solution.py:76
  181.3 0.8 fusion.17
  182.0 0.0 all-gather.8.cloned.1.call-update
  182.1 0.1 reshape.116
  182.2 53.4 %all-gather.8.cloned.1.call-done = bf16[24576,128]{1,0:T(8,128)(2,1)} async-done(((bf16[768,128]{1,0:T(8,128)(2,1)}), bf16[24576,128]{1,0:T(8,128)(2,1)}) %all-gather.8.cloned.1.call-update) | async-done | bytes 6291472 | tf_op jit(solution)/shard_map/all_gather | solution.py:84
  235.5 5.5 %gather_fusion.4 = bf16[96,128,128]{2,1,0:T(8,128)(2,1)} fusion(bf16[192,128,128]{2,1,0:T(8,128)(2,1)} %bitcast.58, s32[1024]{0:T(1024)S(1)} %pad_clamp_fusion), kind=kCustom, calls=%fused_computation.4 | custom fusion | bytes 6291840 | tf_op jit(solution)/shard_map/gather | solution.py:71
  241.0 3.9 %convert_reduce_fusion = f32[6,128,128]{2,1,0:T(8,128)S(1)} fusion(f32[8,6,128]{2,1,0:T(8,128)S(1)} %fusion.21, bf16[8,6,128,256]{3,2,1,0:T(8,128)(2,1)} %bitcast.67, bf16[6,8,256,128]{3,2,1,0:T(8,128)(2,1)} %bitcast.55), kind=kOutput, calls=%fused_computation.11 | convolution fusion | flops 405700608 | bytes 6709248 | tf_op jit(solution)/shard_map/gtmk,tgkc->gtmc/dot_general | solution.py:76
  244.9 0.7 fusion.16
  (16 shorter events, 0.2 us)
Async XLA Ops:
  6.5 28.0 %copy-start = (bf16[768,1000]{0,1:T(8,128)(2,1)S(1)}, bf16[768,1000]{0,1:T(8,128)(2,1)}, u32[]{:S(2)}) copy-start(bf16[768,1000]{0,1:T(8,128)(2,1)} %param.6) | copy-start | bytes 4608004
  29.2 6.4 %copy-start.2 = (s32[768,50]{0,1:T(8,128)S(1)}, s32[768,50]{0,1:T(8,128)}, u32[]{:S(2)}) copy-start(s32[768,50]{0,1:T(8,128)} %param.9) | copy-start | bytes 460804
  29.2 14.0 %copy-start.3 = (f32[768]{0:T(1024)S(1)}, f32[768]{0:T(1024)}, u32[]{:S(2)}) copy-start(f32[768]{0:T(1024)} %param.7) | copy-start | bytes 9220
  29.2 82.3 %all-to-all-start.1 = ((bf16[32,128,768]{2,1,0:T(8,128)(2,1)}), bf16[32,128,768]{2,1,0:T(8,128)(2,1)}, u32[]{:S(2)}, u32[]{:S(2)}) async-start(bf16[32,128,768]{2,1,0:T(8,128)(2,1)} %gather_fusion), calls=%async_computation.1 | async-start | bytes 12582912 | tf_op jit(solution)/shard_map/all_to_all | solution.py:49
  34.5 94.6 %all-gather.6.cloned.1.call-start = ((), (), s32[]{:S(2)}) async-start(), calls=%async_computation.2 | async-start | bytes 3342336 | tf_op jit(solution)/shard_map/all_gather | solution.py:16
  34.8 82.0 %copy-start.1 = (bf16[768,768]{1,0:T(8,128)(2,1)S(1)}, bf16[768,768]{1,0:T(8,128)(2,1)}, u32[]{:S(2)}) copy-start(bf16[768,768]{1,0:T(8,128)(2,1)} %param.5) | copy-start | bytes 3538948
  35.6 139.8 %all-gather.10.cloned.1.call-start = ((), (), s32[]{:S(2)}) async-start(), calls=%async_computation.4 | async-start | bytes 3538944 | tf_op jit(solution)/shard_map/all_gather | solution.py:61
  120.5 115.1 %all-gather.8.cloned.1.call-start = ((), (), s32[]{:S(2)}) async-start(), calls=%async_computation.3 | async-start | bytes 6488064 | tf_op jit(solution)/shard_map/all_gather | solution.py:84
  129.1 28.5 %collective-permute-start = (bf16[96,128,128]{2,1,0:T(8,128)(2,1)}, bf16[96,128,128]{2,1,0:T(8,128)(2,1)}, u32[]{:S(2)}, u32[]{:S(2)}) collective-permute-start(bf16[96,128,128]{2,1,0:T(8,128)(2,1)} %bitcast.51), channel_id=1, source_target_pairs={{0,1},{1,0},{2,3},{3,2},{4,5},{5,4},{6,7},{7,6},{8,9},{9,8},{10,11... | collective-permute-start | bytes 9437192 | tf_op jit(solution)/shard_map/ppermute | solution.py:17
Sparse Core Ops, SparseCore 0:
  37.7 91.3 all-gather.5
  130.9 44.4 all-gather.9
  182.2 53.3 all-gather.7
where the time goes:
time: 253 us; the launch traced here: 252 us
  waiting for transfers between devices  143 us (57%)
  blocking collectives  37.7 us (15%)
  local copies, waits for them, and re-layouts  27.4 us (11%)
  between operations  13.3 us (5%)
  matrix products  12.2 us (5%)
  other arithmetic  11.5 us (5%)
  starting transfers between devices  6.68 us (3%)
    all_to_all x1, waiting for transfers between devices, body(): lax.all_to_all(send_emb, COL, split_axis=0, concat_axis=0, tiled=True)  68.2 us
    all_gather x1, waiting for transfers between devices, body(): lax.all_gather(spread, COL, tiled=True).reshape(-1, BLOCK, lanes)  53.4 us
    all_gather x1, blocking collectives, body(): stats = lax.all_gather(jnp.stack([local_max, local_sum]), 'row')  22.3 us
    all_to_all x1, blocking collectives, body(): lax.all_to_all(wanted, COL, split_axis=0, concat_axis=0, tiled=True)  15.3 us
    all_gather x1, waiting for transfers between devices, body(): all_weights = lax.all_gather(local_weights, 'row')  13.1 us
    dot_general x2, matrix products, propagate_using(): jnp.einsum('gtmk,tgkc->gtmc', all_weights, candidates, preferred_element_...  9.73 us
    all_gather x1, waiting for transfers between devices, gather_columns(): same_core = lax.all_gather(x, 'chip', tiled=True).reshape(-1, BLOCK, width)  8.61 us
    reduce_or x1, other arithmetic, body(): in_mask = jnp.any(shifted[:, :, None] == positions[None, None, :], axis=1)  7.22 us
  transfers between devices with their start and end apart: 5, of which 4 were waited for; matrix products, arithmetic and copies ran while one was open for 11% of the time, Pallas kernels for 0%

commit v1 on v0

--- a/solution.py
+++ b/solution.py
@@ -13,7 +13,9 @@
 
 def gather_columns(x):
     rows_here, width = x.shape
-    same_core = lax.all_gather(x, "chip", tiled=True).reshape(-1, BLOCK, width)
+    same_core = jnp.concatenate(
+        lax.all_to_all(jnp.stack([x] * lax.axis_size("chip")), "chip", 0, 0), axis=0
+    ).reshape(-1, BLOCK, width)
     other_core = lax.ppermute(same_core, "core", [(0, 1), (1, 0)])
     return (same_core, other_core)
 

time: 253 us -> 276 us (1.091)
  waiting for transfers between devices: 143 us -> 156 us
  starting transfers between devices: 6.68 us -> 16 us
    all_to_all x0 -> x1, waiting for transfers between devices: none -> 26.3 us  [gather_columns(): lax.all_to_all(jnp.stack([x] * lax.axis_size('chip')), 'chip', 0, 0)]
    all_gather x1, waiting for transfers between devices: 13.1 us -> 0.02 us  [body(): all_weights = lax.all_gather(local_weights, 'row')]
    all_gather x1 -> x0, waiting for transfers between devices: 8.61 us -> none  [gather_columns(): same_core = lax.all_gather(x, 'chip', tiled=True).reshape(-1, BLOCK, width)]
    all_to_all x0 -> x1, starting transfers between devices: none -> 7.32 us  [gather_columns(): lax.all_to_all(jnp.stack([x] * lax.axis_size('chip')), 'chip', 0, 0)]
    all_to_all x1, waiting for transfers between devices: 68.2 us -> 73 us  [body(): lax.all_to_all(send_emb, COL, split_axis=0, concat_axis=0, tiled=True)]
  transfers between devices with their start and end apart: 5 -> 5, of which waited for: 4 -> 4; matrix products, arithmetic and copies ran while one was open for 11% -> 9% of each run, Pallas kernels for 0% -> 0%
where the time goes in v1:
time: 276 us
  waiting for transfers between devices  156 us (57%)
  blocking collectives  37.8 us (14%)
  local copies, waits for them, and re-layouts  28.8 us (10%)
  starting transfers between devices  16 us (6%)
  between operations  13.6 us (5%)
  matrix products  12.2 us (4%)
  other arithmetic  11.5 us (4%)
    all_to_all x1, waiting for transfers between devices, body(): lax.all_to_all(send_emb, COL, split_axis=0, concat_axis=0, tiled=True)  73 us
    all_gather x1, waiting for transfers between devices, body(): lax.all_gather(spread, COL, tiled=True).reshape(-1, BLOCK, lanes)  55.9 us
    all_to_all x1, waiting for transfers between devices, gather_columns(): lax.all_to_all(jnp.stack([x] * lax.axis_size('chip')), 'chip', 0, 0)  26.3 us
    all_gather x1, blocking collectives, body(): stats = lax.all_gather(jnp.stack([local_max, local_sum]), 'row')  22.4 us
    all_to_all x1, blocking collectives, body(): lax.all_to_all(wanted, COL, split_axis=0, concat_axis=0, tiled=True)  15.3 us
    dot_general x2, matrix products, propagate_using(): jnp.einsum('gtmk,tgkc->gtmc', all_weights, candidates, preferred_element_...  9.74 us
    all_to_all x1, starting transfers between devices, gather_columns(): lax.all_to_all(jnp.stack([x] * lax.axis_size('chip')), 'chip', 0, 0)  7.32 us
    reduce_or x1, other arithmetic, body(): in_mask = jnp.any(shifted[:, :, None] == positions[None, None, :], axis=1)  7.22 us
  transfers between devices with their start and end apart: 5, of which 4 were waited for; matrix products, arithmetic and copies ran while one was open for 9% of the time, Pallas kernels for 0%

profile of v1, /device:TPU:1, one launch (start us, length us, event | category | flops | bytes accessed | tf_op | source)
XLA Modules:
  0.0 275.9 jit_solution(18244483634525050729)
XLA Ops:
  6.5 0.0 copy-start
  6.5 0.8 fusion.23
  7.4 0.7 compare_select_fusion.1
  8.1 0.1 compare_select_fusion.3
  8.1 0.1 fusion.22
  8.2 0.1 copy.42
  8.3 15.3 %all_to_all.22 = s32[32,1,1]{2,1,0:T(1,128)S(1)} all-to-all(s32[32,1,1]{2,1,0:T(1,128)S(1)} %copy.42), channel_id=1, replica_groups=mesh['row'=8,'chip'=16,'core'=2] {'chip','core'}, dimensions={0} | all-to-all | bytes 256 | tf_op jit(solution)/shard_map/all_to_all | solution.py:39
  23.7 0.7 reduce.1
  24.4 4.9 %gather_fusion = bf16[32,128,768]{2,1,0:T(8,128)(2,1)} fusion(bf16[6,128,768]{2,1,0:T(8,128)(2,1)} %bitcast.49, s32[1024]{0:T(1024)S(1)} %pad_clamp_fusion.3), kind=kCustom, calls=%fused_computation | custom fusion | bytes 12583040 | tf_op jit(solution)/shard_map/gather | solution.py:41
  29.2 0.0 copy-start.2
  29.2 5.3 %all-to-all-start.1 = ((bf16[32,128,768]{2,1,0:T(8,128)(2,1)}), bf16[32,128,768]{2,1,0:T(8,128)(2,1)}, u32[]{:S(2)}, u32[]{:S(2)}) async-start(bf16[32,128,768]{2,1,0:T(8,128)(2,1)} %gather_fusion), calls=%async_computation.1 | async-start | bytes 12582912 | tf_op jit(solution)/shard_map/all_to_all | solution.py:51
  34.5 0.0 copy-done
  34.5 0.1 constant_dynamic-slice_fusion
  34.6 0.2 copy.51
  34.8 0.0 copy-done.2
  34.9 73.0 %all-to-all-done.1 = bf16[32,128,768]{2,1,0:T(8,128)(2,1)} async-done(((bf16[32,128,768]{2,1,0:T(8,128)(2,1)}), bf16[32,128,768]{2,1,0:T(8,128)(2,1)}, u32[]{:S(2)}, u32[]{:S(2)}) %all-to-all-start.1) | async-done | bytes 6291488 | tf_op jit(solution)/shard_map/all_to_all | solution.py:51
  107.8 2.3 stack.8
  110.1 7.3 %all-to-all-start.2 = ((bf16[16,768,128]{2,1,0:T(8,128)(2,1)}), bf16[16,768,128]{2,1,0:T(8,128)(2,1)}, u32[]{:S(2)}, u32[]{:S(2)}) async-start(bf16[16,768,128]{2,1,0:T(8,128)(2,1)} %stack.8), calls=%async_computation.2 | async-start | bytes 6291456 | tf_op jit(solution)/shard_map/all_to_all | solution.py:17
  117.4 0.0 copy-start.1
  117.5 0.0 all-gather.7.cloned.1.call-start
  117.5 7.2 %fusion = pred[768,256]{1,0:T(8,128)(4,1)S(1)} fusion(s32[768,50]{0,1:T(8,128)S(1)} %and_select_fusion), kind=kLoop, calls=%fused_computation.6 | loop fusion | flops 19464192 | bytes 350208 | tf_op jit(solution)/shard_map/reduce_or | solution.py:49
  124.7 0.3 copy.44
  125.0 0.1 reshape.90
  125.1 0.0 copy-done.3
  125.1 5.0 %gather_fusion.1 = bf16[12,128,768]{2,1,0:T(8,128)(2,1)} fusion(bf16[32,128,768]{2,1,0:T(8,128)(2,1)} %all-to-all-done.1, s32[1024]{0:T(1024)S(1)} %pad_clamp_fusion.2), kind=kCustom, calls=%fused_computation.1 | custom fusion | bytes 4718640 | tf_op jit(solution)/shard_map/gather | solution.py:52
  130.1 0.0 copy-done.1
  130.1 2.5 select_reduce_fusion
  132.6 0.2 fusion.15
  132.8 1.0 copy.45
  133.7 0.0 all-gather.7.cloned.1.call-update
  133.8 0.0 all-gather.5.cloned.1.call-start
  133.8 26.3 %all-to-all-done.2 = bf16[16,768,128]{2,1,0:T(8,128)(2,1)} async-done(((bf16[16,768,128]{2,1,0:T(8,128)(2,1)}), bf16[16,768,128]{2,1,0:T(8,128)(2,1)}, u32[]{:S(2)}, u32[]{:S(2)}) %all-to-all-start.2) | async-done | bytes 3145760 | tf_op jit(solution)/shard_map/all_to_all | solution.py:17
  160.2 3.3 %collective-permute-start = (bf16[96,128,128]{2,1,0:T(8,128)(2,1)}, bf16[96,128,128]{2,1,0:T(8,128)(2,1)}, u32[]{:S(2)}, u32[]{:S(2)}) collective-permute-start(bf16[96,128,128]{2,1,0:T(8,128)(2,1)} %bitcast.8), channel_id=1, source_target_pairs={{0,1},{1,0},{2,3},{3,2},{4,5},{5,4},{6,7},{7,6},{8,9},{9,8},{10,11... | collective-permute-start | bytes 9437192 | tf_op jit(solution)/shard_map/ppermute | solution.py:19
  163.5 0.1 reshape.98
  163.6 0.1 broadcast_in_dim.63
  163.7 4.6 %gather_fusion.2 = bf16[96,128,128]{2,1,0:T(8,128)(2,1)} fusion(bf16[96,128,128]{2,1,0:T(8,128)(2,1)} %bitcast.8, s32[1024]{0:T(1024)S(1)} %pad_clamp_fusion.1), kind=kCustom, calls=%fused_computation.2 | custom fusion | bytes 6291840 | tf_op jit(solution)/shard_map/gather | solution.py:76
  168.3 0.8 collective-permute-done
  169.1 4.6 %gather_fusion.3 = bf16[96,128,128]{2,1,0:T(8,128)(2,1)} fusion(bf16[96,128,128]{2,1,0:T(8,128)(2,1)} %collective-permute-done, s32[1024]{0:T(1024)S(1)} %pad_clamp_fusion.1), kind=kCustom, calls=%fused_computation.3 | custom fusion | bytes 6291840 | tf_op jit(solution)/shard_map/gather | solution.py:76
  173.7 22.4 %all-gather.1 = f32[16,6,128]{2,1,0:T(8,128)S(1)} all-gather(f32[2,6,128]{2,1,0:T(8,128)S(1)} %pad_maximum_fusion), channel_id=3, replica_groups=mesh['row'=8,'chip'=16,'core'=2] {'row'}, dimensions={0}, use_global_device_ids=true | all-gather | bytes 55296 | tf_op jit(solution)/shard_map/all_gather | solution.py:62
  196.2 0.0 all-gather.7.cloned.1.call-done
  196.3 5.9 %convert_reduce_fusion.1 = f32[6,128,128]{2,1,0:T(8,128)S(1)} fusion(f32[8,6,128]{2,1,0:T(8,128)S(1)} %fusion.21, bf16[8,6,128,256]{3,2,1,0:T(8,128)(2,1)} %bitcast.64, bf16[6,8,256,128]{3,2,1,0:T(8,128)(2,1)} %bitcast.51, bf16[6,8,256,128]{3,2,1,0:T(8,128)(2,1)} %bitcast.52, pred[6,8,256]{2,1,0:T(8,128)(4,1)S(1)} %broadcast_in_dim.64), kind=kOutput, calls=%fused_computation.13 | convolution fusion | flops 407273472 | bytes 9867264 | tf_op jit(solution)/shard_map/gtmk,tgkc->gtmc/dot_general | solution.py:78
  202.2 0.8 fusion.17
  202.9 0.0 all-gather.5.cloned.1.call-update
  203.0 0.1 reshape.114
  203.1 55.9 %all-gather.5.cloned.1.call-done = bf16[24576,128]{1,0:T(8,128)(2,1)} async-done(((bf16[768,128]{1,0:T(8,128)(2,1)}), bf16[24576,128]{1,0:T(8,128)(2,1)}) %all-gather.5.cloned.1.call-update) | async-done | bytes 6291472 | tf_op jit(solution)/shard_map/all_gather | solution.py:86
  259.0 5.5 %gather_fusion.4 = bf16[96,128,128]{2,1,0:T(8,128)(2,1)} fusion(bf16[192,128,128]{2,1,0:T(8,128)(2,1)} %bitcast.56, s32[1024]{0:T(1024)S(1)} %pad_clamp_fusion), kind=kCustom, calls=%fused_computation.4 | custom fusion | bytes 6291840 | tf_op jit(solution)/shard_map/gather | solution.py:73
  264.4 3.9 %convert_reduce_fusion = f32[6,128,128]{2,1,0:T(8,128)S(1)} fusion(f32[8,6,128]{2,1,0:T(8,128)S(1)} %fusion.21, bf16[8,6,128,256]{3,2,1,0:T(8,128)(2,1)} %bitcast.65, bf16[6,8,256,128]{3,2,1,0:T(8,128)(2,1)} %bitcast.53), kind=kOutput, calls=%fused_computation.11 | convolution fusion | flops 405700608 | bytes 6709248 | tf_op jit(solution)/shard_map/gtmk,tgkc->gtmc/dot_general | solution.py:78
  268.3 0.7 fusion.16
  (16 shorter events, 0.2 us)
Async XLA Ops:
  6.5 28.0 %copy-start = (bf16[768,1000]{0,1:T(8,128)(2,1)S(1)}, bf16[768,1000]{0,1:T(8,128)(2,1)}, u32[]{:S(2)}) copy-start(bf16[768,1000]{0,1:T(8,128)(2,1)} %param.6) | copy-start | bytes 4608004
  29.2 5.6 %copy-start.2 = (s32[768,50]{0,1:T(8,128)S(1)}, s32[768,50]{0,1:T(8,128)}, u32[]{:S(2)}) copy-start(s32[768,50]{0,1:T(8,128)} %param.9) | copy-start | bytes 460804
  29.2 78.6 %all-to-all-start.1 = ((bf16[32,128,768]{2,1,0:T(8,128)(2,1)}), bf16[32,128,768]{2,1,0:T(8,128)(2,1)}, u32[]{:S(2)}, u32[]{:S(2)}) async-start(bf16[32,128,768]{2,1,0:T(8,128)(2,1)} %gather_fusion), calls=%async_computation.1 | async-start | bytes 12582912 | tf_op jit(solution)/shard_map/all_to_all | solution.py:51
  110.1 15.0 %copy-start.3 = (f32[768]{0:T(1024)S(1)}, f32[768]{0:T(1024)}, u32[]{:S(2)}) copy-start(f32[768]{0:T(1024)} %param.7) | copy-start | bytes 9220
  110.1 50.0 %all-to-all-start.2 = ((bf16[16,768,128]{2,1,0:T(8,128)(2,1)}), bf16[16,768,128]{2,1,0:T(8,128)(2,1)}, u32[]{:S(2)}, u32[]{:S(2)}) async-start(bf16[16,768,128]{2,1,0:T(8,128)(2,1)} %stack.8), calls=%async_computation.2 | async-start | bytes 6291456 | tf_op jit(solution)/shard_map/all_to_all | solution.py:17
  117.4 12.7 %copy-start.1 = (bf16[768,768]{1,0:T(8,128)(2,1)S(1)}, bf16[768,768]{1,0:T(8,128)(2,1)}, u32[]{:S(2)}) copy-start(bf16[768,768]{1,0:T(8,128)(2,1)} %param.5) | copy-start | bytes 3538948
  117.5 78.8 %all-gather.7.cloned.1.call-start = ((), (), s32[]{:S(2)}) async-start(), calls=%async_computation.4 | async-start | bytes 3538944 | tf_op jit(solution)/shard_map/all_gather | solution.py:63
  133.8 125.2 %all-gather.5.cloned.1.call-start = ((), (), s32[]{:S(2)}) async-start(), calls=%async_computation.3 | async-start | bytes 6488064 | tf_op jit(solution)/shard_map/all_gather | solution.py:86
  160.2 9.0 %collective-permute-start = (bf16[96,128,128]{2,1,0:T(8,128)(2,1)}, bf16[96,128,128]{2,1,0:T(8,128)(2,1)}, u32[]{:S(2)}, u32[]{:S(2)}) collective-permute-start(bf16[96,128,128]{2,1,0:T(8,128)(2,1)} %bitcast.8), channel_id=1, source_target_pairs={{0,1},{1,0},{2,3},{3,2},{4,5},{5,4},{6,7},{7,6},{8,9},{9,8},{10,11... | collective-permute-start | bytes 9437192 | tf_op jit(solution)/shard_map/ppermute | solution.py:19
Sparse Core Ops, SparseCore 0:
  133.9 49.0 all-gather.6
  203.1 55.8 all-gather.4
